TPU v7x, 256 devices: a whole 4x4x8 slice. The times are simulated.
256 devices in a mesh: layer: 32 (over z, y), plane: 8 (over x, core).
Axes of the slice: x: 4, y: 4, z: 8, core: 2. Of those that a mesh axis runs over, the one named last changes fastest.
Arguments:
- rhs_field: float32 [32, 2, 4, 64, 1024], P('layer', None, None, None, 'plane'), may hold values from -6 to 6
- panel_inverse: bfloat16 [32, 1024, 2048], P('layer'), may hold values from -1 to 1
- coupling: float32 [32, 2, 4, 64], P('layer', None, None, 'plane'), may hold values from -0.98 to 0.98, as said below
Outputs:
- sweep_field: float32 [32, 2, 4, 64, 1024], P('layer', None, None, None, 'plane')
Inputs may be any that keep to these rules, and one draw needn't show every extreme that they name: Every complex coupling has modulus at most 0.98.
All inputs are finite; a program needn't handle non-finite values.
Results may differ from a plain program's by a relative error of at most 0.025.
Values may be sent and summed in bfloat16 or wider, within the bound.
No kernel may reach another device: no remote copies, remote signals or barrier semaphores. Data moves between devices by JAX's collectives and lax.ppermute only.
A program may use at most 64 MiB of HBM per device.

v0:
```python
import jax
import jax.numpy as jnp
from jax import lax
from jax.sharding import PartitionSpec as P


def complex_product(rows, inverse, width):
    flat = rows.reshape(-1, width)
    product = jnp.dot(flat, inverse, preferred_element_type=jnp.float32)
    product = product.reshape(rows.shape[:-1] + (2 * width,))
    real = product[0, ..., :width] - product[1, ..., width:]
    imag = product[0, ..., width:] + product[1, ..., :width]
    return jnp.stack([real, imag])


def twist(factor, field):
    real = factor[0] * field[0] - factor[1] * field[1]
    imag = factor[0] * field[1] + factor[1] * field[0]
    return jnp.stack([real, imag])


def body(rhs_field, panel_inverse, coupling):
    lines = lax.all_to_all(rhs_field, "plane", split_axis=3, concat_axis=4, tiled=True)[0]
    inverse = panel_inverse[0]
    factors = coupling[0][..., None]
    width = inverse.shape[0]
    layers = lax.axis_size("layer")
    planes = lax.axis_size("plane")
    place = lax.axis_index("layer")
    plane = lax.axis_index("plane")
    pairs = layers // 2
    down = [(2 * j + 1, 2 * j) for j in range(pairs)]
    ahead = [(2 * j, 2 * j + 2) for j in range(pairs - 1)]
    behind = [(2 * j + 2, 2 * j) for j in range(pairs - 1)]
    back = [(2 * j, 2 * j + 1) for j in range(pairs)]
    rows = width // planes
    piece = lax.dynamic_slice_in_dim(inverse, plane * rows, rows, 0)
    piece = lax.ppermute(piece, "layer", down)
    inverse_next = lax.all_gather(piece, "plane", axis=0, tiled=True)
    lines_next = lax.ppermute(lines, "layer", down)
    factors_next = lax.ppermute(factors, "layer", down)

    def pair_forward(incoming):
        mixed = (lines + twist(factors, incoming.astype(jnp.float32))).astype(jnp.bfloat16)
        first = complex_product(mixed, inverse, width)
        carried = first.astype(jnp.bfloat16).astype(jnp.float32)
        mixed = (lines_next + twist(factors_next, carried)).astype(jnp.bfloat16)
        second = complex_product(mixed, inverse_next, width)
        return (first, second)

    first, second = pair_forward(jnp.zeros(lines.shape, jnp.bfloat16))
    valid = place == 0
    store_a = jnp.where(valid, first, 0.0)
    store_b = jnp.where(valid, second, 0.0)

    def forward(section, carry):
        store_a, store_b, outgoing = carry
        incoming = lax.ppermute(outgoing, "layer", ahead)
        first, second = pair_forward(incoming)
        valid = place == 2 * section
        store_a = jnp.where(valid, first, store_a)
        store_b = jnp.where(valid, second, store_b)
        return (store_a, store_b, second.astype(jnp.bfloat16))

    store_a, store_b, _ = lax.fori_loop(
        1, pairs, forward, (store_a, store_b, second.astype(jnp.bfloat16))
    )

    def pair_backward(sweep_b):
        carried = twist(factors_next, sweep_b).astype(jnp.bfloat16)
        sweep_a = store_a + complex_product(carried, inverse, width)
        return (sweep_a, twist(factors, sweep_a).astype(jnp.bfloat16))

    sweep_b = store_b
    sweep_a, outgoing = pair_backward(sweep_b)
    valid = place == layers - 2
    result_a = jnp.where(valid, sweep_a, 0.0)
    result_b = jnp.where(valid, sweep_b, 0.0)

    def backward(section, carry):
        result_a, result_b, outgoing = carry
        incoming = lax.ppermute(outgoing, "layer", behind)
        sweep_b = store_b + complex_product(incoming, inverse_next, width)
        sweep_a, outgoing = pair_backward(sweep_b)
        valid = place == layers - 2 - 2 * section
        result_a = jnp.where(valid, sweep_a, result_a)
        result_b = jnp.where(valid, sweep_b, result_b)
        return (result_a, result_b, outgoing)

    result_a, result_b, _ = lax.fori_loop(1, pairs, backward, (result_a, result_b, outgoing))
    returned = lax.ppermute(result_b, "layer", back)
    result = jnp.where(place % 2 == 0, result_a, returned)
    return lax.all_to_all(result[None], "plane", split_axis=4, concat_axis=3, tiled=True)


def solution(mesh):
    in_specs = (
        P("layer", None, None, None, "plane"),
        P("layer", None, None),
        P("layer", None, None, "plane"),
    )
    out_specs = P("layer", None, None, None, "plane")
    return jax.shard_map(body, mesh=mesh, in_specs=in_specs, out_specs=out_specs, check_vma=False)
```

profile of v0, /device:TPU:120, one launch (start us, length us, event | category | flops | bytes accessed | tf_op | source)
XLA Modules:
  0.0 568.8 jit_solution(8651485035003527377)
XLA Ops:
  7.6 2.7 collective-permute-start.4
  10.3 11.1 %collective-permute-done.4 = bf16[128,2048]{1,0:T(8,128)(2,1)S(1)} collective-permute-done((bf16[128,2048]{1,0:T(8,128)(2,1)S(1)}, bf16[128,2048]{1,0:T(8,128)(2,1)S(1)}, u32[]{:S(2)}, u32[]{:S(2)}) %collective-permute-start.4) | collective-permute-done | bytes 524320 | tf_op jit(solution)/shard_map/ppermute | solution.py:38
  22.3 1.8 copy.17
  24.1 4.3 all-to-all-start
  28.4 4.4 collective-permute-start.3
  36.0 4.4 collective-permute-start.2
  40.5 3.0 fusion.27
  45.5 14.8 %all-gather.2.cloned.1.call-done = bf16[1024,2048]{1,0:T(8,128)(2,1)} async-done(((bf16[128,2048]{1,0:T(8,128)(2,1)}), bf16[1024,2048]{1,0:T(8,128)(2,1)}) %all-gather.2.cloned.1.call-update) | async-done | bytes 4194320 | tf_op jit(solution)/shard_map/all_gather | solution.py:39
  60.3 3.0 fusion.23
  63.5 80.7 %while.34 = (s32[]{:T(128)}, f32[2,4,8,1024]{3,2,1,0:T(8,128)S(1)}, f32[2,4,8,1024]{3,2,1,0:T(8,128)S(1)}, bf16[2,4,8,1024]{3,2,1,0:T(8,128)(2,1)S(1)}, s32[]{:T...) while((s32[]{:T(128)}, f32[2,4,8,1024]{3,2,1,0:T(8,128)S(1)}, ...), condition=%wide.region_1.2_spmd, body=%wide.region_0.1_spmd.sunk | while | flops 538312704 | bytes 33294036 | solution.py:65
  64.3 3.2 fusion.65
  69.7 3.2 fusion.65
  75.1 3.2 fusion.65
  80.5 3.2 fusion.65
  85.9 3.2 fusion.65
  91.3 3.2 fusion.65
  96.6 3.2 fusion.65
  102.0 3.2 fusion.65
  107.4 3.2 fusion.65
  112.8 3.2 fusion.65
  118.2 3.2 fusion.65
  123.5 3.2 fusion.65
  128.9 3.2 fusion.65
  134.3 3.2 fusion.65
  139.7 3.2 fusion.65
  144.3 3.0 fusion.25
  147.6 80.6 %while.35 = (s32[]{:T(128)}, f32[2,4,8,1024]{3,2,1,0:T(8,128)S(1)}, f32[2,4,8,1024]{3,2,1,0:T(8,128)S(1)}, bf16[2,4,8,1024]{3,2,1,0:T(8,128)(2,1)S(1)}, s32[]{:T...) while((s32[]{:T(128)}, f32[2,4,8,1024]{3,2,1,0:T(8,128)S(1)}, ...), condition=%wide.region_3.4_spmd, body=%wide.region_2.3_spmd.sunk | while | flops 538050560 | bytes 32245480 | solution.py:90
  148.3 3.2 fusion.74
  153.7 3.2 fusion.74
  159.1 3.2 fusion.74
  164.4 3.2 fusion.74
  169.8 3.2 fusion.74
  175.2 3.2 fusion.74
  180.6 3.2 fusion.74
  185.9 3.2 fusion.74
  191.3 3.2 fusion.74
  196.7 3.2 fusion.74
  202.1 3.2 fusion.74
  207.4 3.2 fusion.74
  212.8 3.2 fusion.74
  218.2 3.2 fusion.74
  223.5 3.2 fusion.74
  229.5 299.4 %collective-permute-done.5 = f32[2,4,8,1024]{3,2,1,0:T(8,128)S(1)} collective-permute-done((f32[2,4,8,1024]{3,2,1,0:T(8,128)S(1)}, f32[2,4,8,1024]{3,2,1,0:T(8,128)S(1)}, u32[]{:S(2)}, u32[]{:S(2)}) %collective-permute-start.5) | collective-permute-done | bytes 262176 | tf_op jit(solution)/shard_map/ppermute | solution.py:91
  529.0 3.1 copy.23
  532.0 6.5 %reshape.75 = f32[8,1,8192]{2,1,0:T(1,128)S(1)} reshape(f32[1024,1,2,4,8]{4,3,2,1,0:T(4,128)} %bitcast.114) | data formatting | bytes 524288
  538.6 10.3 %all_to_all.33 = f32[8,1,8192]{2,1,0:T(1,128)S(1)} all-to-all(f32[8,1,8192]{2,1,0:T(1,128)S(1)} %reshape.75), channel_id=1, replica_groups=mesh['layer'=32,'plane'=8] {'plane'}, dimensions={0} | all-to-all | bytes 524288 | tf_op jit(solution)/shard_map/all_to_all | solution.py:93
  550.6 6.9 %reshape.76 = f32[1024,1,2,4,8]{4,3,2,1,0:T(4,128)} reshape(f32[8,8192]{1,0:T(8,128)S(1)} %reduce) | data formatting | bytes 524288
  557.5 4.4 copy.24
  (452 shorter events, 72.8 us)
Async XLA Ops:
  6.5 53.8 %all-gather.2.cloned.1.call-start = ((), (), s32[]{:S(2)}) async-start(), calls=%async_computation.2 | async-start | bytes 4718592 | tf_op jit(solution)/shard_map/all_gather | solution.py:39
  7.6 13.8 %collective-permute-start.4 = (bf16[128,2048]{1,0:T(8,128)(2,1)S(1)}, bf16[128,2048]{1,0:T(8,128)(2,1)S(1)}, u32[]{:S(2)}, u32[]{:S(2)}) collective-permute-start(bf16[128,2048]{1,0:T(8,128)(2,1)S(1)} %dynamic-slice_bitcast_fusion), channel_id=1, source_target_pairs={{8,0},{24,16},{40,32},{56,48},{72,64},{88,80},{104,96},{120,112},{... | collective-permute-start | bytes 1572872 | tf_op jit(solution)/shard_map/ppermute | solution.py:38
  24.1 11.8 %all-to-all-start = ((f32[1,2,4,64,128]{4,2,1,0,3:T(4,128)}), f32[1,2,4,64,128]{4,2,1,0,3:T(4,128)S(1)}, u32[]{:S(2)}, u32[]{:S(2)}) async-start(f32[1,2,4,64,128]{4,2,1,0,3:T(4,128)} %copy.17), calls=%async_computation | async-start | bytes 524288 | tf_op jit(solution)/shard_map/all_to_all | solution.py:23
  28.4 5.9 %collective-permute-start.3 = (f32[2,4,8,1]{2,1,0,3:T(4,128)}, f32[2,4,8,1]{2,1,0,3:T(4,128)S(1)}, u32[]{:S(2)}, u32[]{:S(2)}) collective-permute-start(f32[2,4,8,1]{2,1,0,3:T(4,128)} %bitcast.120), channel_id=1, source_target_pairs={{8,0},{24,16},{40,32},{56,48},{72,64},{88,80},{104,96},{120,112},{... | collective-permute-start | bytes 776 | tf_op jit(solution)/shard_map/ppermute | solution.py:41
  36.0 9.6 %collective-permute-start.2 = (f32[2,4,8,1024]{3,2,1,0:T(8,128)S(1)}, f32[2,4,8,1024]{3,2,1,0:T(8,128)S(1)}, u32[]{:S(2)}, u32[]{:S(2)}) collective-permute-start(f32[2,4,8,1024]{3,2,1,0:T(8,128)S(1)} %bitcast.116), channel_id=1, source_target_pairs={{8,0},{24,16},{40,32},{56,48},{72,64},{88,80},{104,96},{120,112},{... | collective-permute-start | bytes 786440 | tf_op jit(solution)/shard_map/ppermute | solution.py:40
  43.6 19.8 %copy-start.2 = (f32[1,2,4,8]{3,2,1,0:T(4,128)S(1)}, f32[1,2,4,8]{3,2,1,0:T(4,128)}, u32[]{:S(2)}) copy-start(f32[1,2,4,8]{3,2,1,0:T(4,128)} %param.9) | copy-start | bytes 772
  63.5 0.7 collective-permute-start
  68.9 0.7 collective-permute-start
  74.2 0.7 collective-permute-start
  79.6 0.7 collective-permute-start
  85.0 0.7 collective-permute-start
  90.4 0.7 collective-permute-start
  95.8 0.7 collective-permute-start
  101.2 0.7 collective-permute-start
  106.5 0.7 collective-permute-start
  111.9 0.7 collective-permute-start
  117.3 0.7 collective-permute-start
  122.7 0.7 collective-permute-start
  128.1 0.7 collective-permute-start
  133.4 0.7 collective-permute-start
  138.8 0.7 collective-permute-start
  147.6 0.7 collective-permute-start.1
  148.3 3.5 copy-start
  153.0 0.7 collective-permute-start.1
  153.7 3.5 copy-start
  158.4 0.7 collective-permute-start.1
  159.1 3.5 copy-start
  163.7 0.7 collective-permute-start.1
  164.4 3.5 copy-start
  169.1 0.7 collective-permute-start.1
  169.8 3.5 copy-start
  174.5 0.7 collective-permute-start.1
  175.2 3.5 copy-start
  179.8 0.7 collective-permute-start.1
  180.6 3.5 copy-start
  185.2 0.7 collective-permute-start.1
  185.9 3.5 copy-start
  190.6 0.7 collective-permute-start.1
  191.3 3.5 copy-start
  196.0 0.7 collective-permute-start.1
  196.7 3.5 copy-start
  201.3 0.7 collective-permute-start.1
  206.7 0.7 collective-permute-start.1
  212.1 0.7 collective-permute-start.1
  217.5 0.7 collective-permute-start.1
  218.2 3.5 copy-start
  222.8 0.7 collective-permute-start.1
  228.2 300.8 %collective-permute-start.5 = (f32[2,4,8,1024]{3,2,1,0:T(8,128)S(1)}, f32[2,4,8,1024]{3,2,1,0:T(8,128)S(1)}, u32[]{:S(2)}, u32[]{:S(2)}) collective-permute-start(f32[2,4,8,1024]{3,2,1,0:T(8,128)S(1)} %get-tuple-element.378), channel_id=1, source_target_pairs={{0,8},{16,24},{32,40},{48,56},{64,72},{80,88},{96,104},{112,120},{... | collective-permute-start | bytes 786440 | tf_op jit(solution)/shard_map/ppermute | solution.py:91
  (20 other events, 66.5 us)
Sparse Core Ops, SparseCore 0:
  22.4 37.9 all-gather.1
where the time goes:
time: 570 us; the launch traced here: 569 us
  waiting for transfers between devices  329 us (58%)
  matrix products  130 us (23%)
  starting transfers between devices  37.1 us (7%)
  local copies, waits for them, and re-layouts  27.3 us (5%)
  other arithmetic  17.9 us (3%)
  between operations  13.6 us (2%)
  blocking collectives  10.3 us (2%)
    ppermute x1, waiting for transfers between devices, body(): returned = lax.ppermute(result_b, 'layer', back)  299 us
    dot_general x63, matrix products, complex_product(): product = jnp.dot(flat, inverse, preferred_element_type=jnp.float32)  130 us
    unnamed x7, local copies, waits for them, and re-layouts  16.1 us
    all_gather x1, waiting for transfers between devices, body(): inverse_next = lax.all_gather(piece, 'plane', axis=0, tiled=True)  14.8 us
  transfers between devices with their start and end apart: 36, of which 6 were waited for; matrix products, arithmetic and copies ran while one was open for 1% of the time, Pallas kernels for 0%

commit v1 on v0

--- a/solution.py
+++ b/solution.py
@@ -90,7 +90,12 @@
     result_a, result_b, _ = lax.fori_loop(1, pairs, backward, (result_a, result_b, outgoing))
     returned = lax.ppermute(result_b, "layer", back)
     result = jnp.where(place % 2 == 0, result_a, returned)
-    return lax.all_to_all(result[None], "plane", split_axis=4, concat_axis=3, tiled=True)
+    return jnp.concatenate(
+        lax.all_to_all(
+            jnp.stack(jnp.split(result[None], lax.axis_size("plane"), 4), axis=0), "plane", 0, 0
+        ),
+        3,
+    )
 
 
 def solution(mesh):

time: 570 us -> 548 us (0.961)
  local copies, waits for them, and re-layouts: 27.3 us -> 6.62 us
    unnamed x7 -> x12, local copies, waits for them, and re-layouts: 16.1 us -> 2.67 us
where the time goes in v1:
time: 548 us; the launch traced here: 547 us
  waiting for transfers between devices  329 us (60%)
  matrix products  130 us (24%)
  starting transfers between devices  37.1 us (7%)
  other arithmetic  16.7 us (3%)
  between operations  13.6 us (2%)
  blocking collectives  10.2 us (2%)
  local copies, waits for them, and re-layouts  6.62 us (1%)
    ppermute x1, waiting for transfers between devices, body(): returned = lax.ppermute(result_b, 'layer', back)  299 us
    dot_general x63, matrix products, complex_product(): product = jnp.dot(flat, inverse, preferred_element_type=jnp.float32)  130 us
    all_gather x1, waiting for transfers between devices, body(): inverse_next = lax.all_gather(piece, 'plane', axis=0, tiled=True)  14.8 us
    ppermute x1, waiting for transfers between devices, body(): piece = lax.ppermute(piece, 'layer', down)  11.1 us
  transfers between devices with their start and end apart: 36, of which 6 were waited for; matrix products, arithmetic and copies ran while one was open for 1% of the time, Pallas kernels for 0%

profile of v1, /device:TPU:120, one launch (start us, length us, event | category | flops | bytes accessed | tf_op | source)
XLA Modules:
  0.0 546.9 jit_solution(14924563763086433845)
XLA Ops:
  6.5 1.1 dynamic-slice_bitcast_fusion
  7.6 2.7 collective-permute-start.4
  10.3 11.1 %collective-permute-done.4 = bf16[128,2048]{1,0:T(8,128)(2,1)S(1)} collective-permute-done((bf16[128,2048]{1,0:T(8,128)(2,1)S(1)}, bf16[128,2048]{1,0:T(8,128)(2,1)S(1)}, u32[]{:S(2)}, u32[]{:S(2)}) %collective-permute-start.4) | collective-permute-done | bytes 524320 | tf_op jit(solution)/shard_map/ppermute | solution.py:38
  22.3 1.8 copy.9
  24.1 4.3 all-to-all-start
  28.4 4.4 collective-permute-start.3
  34.3 1.6 all-to-all-done
  35.9 4.4 collective-permute-start.2
  40.5 3.0 fusion.27
  43.8 1.8 collective-permute-done.2
  45.5 14.8 %all-gather.2.cloned.1.call-done = bf16[1024,2048]{1,0:T(8,128)(2,1)} async-done(((bf16[128,2048]{1,0:T(8,128)(2,1)}), bf16[1024,2048]{1,0:T(8,128)(2,1)}) %all-gather.2.cloned.1.call-update) | async-done | bytes 4194320 | tf_op jit(solution)/shard_map/all_gather | solution.py:39
  60.3 3.0 fusion.23
  63.5 80.7 %while.34 = (s32[]{:T(128)}, f32[2,4,8,1024]{3,2,1,0:T(8,128)S(1)}, f32[2,4,8,1024]{3,2,1,0:T(8,128)S(1)}, bf16[2,4,8,1024]{3,2,1,0:T(8,128)(2,1)S(1)}, s32[]{:T...) while((s32[]{:T(128)}, f32[2,4,8,1024]{3,2,1,0:T(8,128)S(1)}, ...), condition=%wide.region_1.2_spmd, body=%wide.region_0.1_spmd.sunk | while | flops 538312704 | bytes 33294036 | solution.py:65
  64.3 3.2 fusion.74
  69.7 3.2 fusion.74
  75.1 3.2 fusion.74
  80.5 3.2 fusion.74
  85.9 3.2 fusion.74
  91.2 3.2 fusion.74
  96.6 3.2 fusion.74
  102.0 3.2 fusion.74
  107.4 3.2 fusion.74
  112.8 3.2 fusion.74
  118.2 3.2 fusion.74
  123.5 3.2 fusion.74
  128.9 3.2 fusion.74
  134.3 3.2 fusion.74
  139.7 3.2 fusion.74
  144.3 3.0 fusion.25
  147.6 80.6 %while.35 = (s32[]{:T(128)}, f32[2,4,8,1024]{3,2,1,0:T(8,128)S(1)}, f32[2,4,8,1024]{3,2,1,0:T(8,128)S(1)}, bf16[2,4,8,1024]{3,2,1,0:T(8,128)(2,1)S(1)}, s32[]{:T...) while((s32[]{:T(128)}, f32[2,4,8,1024]{3,2,1,0:T(8,128)S(1)}, ...), condition=%wide.region_3.4_spmd, body=%wide.region_2.3_spmd.sunk | while | flops 538050560 | bytes 32245480 | solution.py:90
  148.3 3.2 fusion.83
  153.7 3.2 fusion.83
  159.1 3.2 fusion.83
  164.4 3.2 fusion.83
  169.8 3.2 fusion.83
  175.2 3.2 fusion.83
  180.6 3.2 fusion.83
  185.9 3.2 fusion.83
  191.3 3.2 fusion.83
  196.7 3.2 fusion.83
  202.0 3.2 fusion.83
  207.4 3.2 fusion.83
  212.8 3.2 fusion.83
  218.2 3.2 fusion.83
  223.5 3.2 fusion.83
  228.2 1.3 collective-permute-start.5
  229.5 299.4 %collective-permute-done.5 = f32[2,4,8,1024]{3,2,1,0:T(8,128)S(1)} collective-permute-done((f32[2,4,8,1024]{3,2,1,0:T(8,128)S(1)}, f32[2,4,8,1024]{3,2,1,0:T(8,128)S(1)}, u32[]{:S(2)}, u32[]{:S(2)}) %collective-permute-start.5) | collective-permute-done | bytes 262176 | tf_op jit(solution)/shard_map/ppermute | solution.py:91
  529.1 10.2 %all_to_all.20 = f32[8,1,2,4,8,128]{5,4,3,2,1,0:T(8,128)S(1)} all-to-all(f32[8,1,2,4,8,128]{5,4,3,2,1,0:T(8,128)S(1)} %fusion.42), channel_id=1, replica_groups=mesh['layer'=32,'plane'=8] {'plane'}, dimensions={0} | all-to-all | bytes 524288 | tf_op jit(solution)/shard_map/all_to_all | solution.py:94
  (455 shorter events, 66.1 us)
Async XLA Ops:
  6.5 53.8 %all-gather.2.cloned.1.call-start = ((), (), s32[]{:S(2)}) async-start(), calls=%async_computation.2 | async-start | bytes 4718592 | tf_op jit(solution)/shard_map/all_gather | solution.py:39
  7.6 13.8 %collective-permute-start.4 = (bf16[128,2048]{1,0:T(8,128)(2,1)S(1)}, bf16[128,2048]{1,0:T(8,128)(2,1)S(1)}, u32[]{:S(2)}, u32[]{:S(2)}) collective-permute-start(bf16[128,2048]{1,0:T(8,128)(2,1)S(1)} %dynamic-slice_bitcast_fusion), channel_id=1, source_target_pairs={{8,0},{24,16},{40,32},{56,48},{72,64},{88,80},{104,96},{120,112},{... | collective-permute-start | bytes 1572872 | tf_op jit(solution)/shard_map/ppermute | solution.py:38
  24.1 11.8 %all-to-all-start = ((f32[1,2,4,64,128]{4,2,1,0,3:T(4,128)}), f32[1,2,4,64,128]{4,2,1,0,3:T(4,128)S(1)}, u32[]{:S(2)}, u32[]{:S(2)}) async-start(f32[1,2,4,64,128]{4,2,1,0,3:T(4,128)} %copy.9), calls=%async_computation | async-start | bytes 524288 | tf_op jit(solution)/shard_map/all_to_all | solution.py:23
  28.4 5.9 %collective-permute-start.3 = (f32[2,4,8,1]{2,1,0,3:T(4,128)}, f32[2,4,8,1]{2,1,0,3:T(4,128)S(1)}, u32[]{:S(2)}, u32[]{:S(2)}) collective-permute-start(f32[2,4,8,1]{2,1,0,3:T(4,128)} %bitcast.149), channel_id=1, source_target_pairs={{8,0},{24,16},{40,32},{56,48},{72,64},{88,80},{104,96},{120,112},{... | collective-permute-start | bytes 776 | tf_op jit(solution)/shard_map/ppermute | solution.py:41
  35.9 9.6 %collective-permute-start.2 = (f32[2,4,8,1024]{3,2,1,0:T(8,128)S(1)}, f32[2,4,8,1024]{3,2,1,0:T(8,128)S(1)}, u32[]{:S(2)}, u32[]{:S(2)}) collective-permute-start(f32[2,4,8,1024]{3,2,1,0:T(8,128)S(1)} %bitcast.145), channel_id=1, source_target_pairs={{8,0},{24,16},{40,32},{56,48},{72,64},{88,80},{104,96},{120,112},{... | collective-permute-start | bytes 786440 | tf_op jit(solution)/shard_map/ppermute | solution.py:40
  43.6 19.8 %copy-start.2 = (f32[1,2,4,8]{3,2,1,0:T(4,128)S(1)}, f32[1,2,4,8]{3,2,1,0:T(4,128)}, u32[]{:S(2)}) copy-start(f32[1,2,4,8]{3,2,1,0:T(4,128)} %param.9) | copy-start | bytes 772
  63.5 0.7 collective-permute-start
  68.9 0.7 collective-permute-start
  74.2 0.7 collective-permute-start
  79.6 0.7 collective-permute-start
  85.0 0.7 collective-permute-start
  90.4 0.7 collective-permute-start
  95.8 0.7 collective-permute-start
  101.1 0.7 collective-permute-start
  106.5 0.7 collective-permute-start
  111.9 0.7 collective-permute-start
  117.3 0.7 collective-permute-start
  122.7 0.7 collective-permute-start
  128.1 0.7 collective-permute-start
  133.4 0.7 collective-permute-start
  138.8 0.7 collective-permute-start
  147.6 0.7 collective-permute-start.1
  148.3 3.5 copy-start
  153.0 0.7 collective-permute-start.1
  153.7 3.5 copy-start
  158.3 0.7 collective-permute-start.1
  159.1 3.5 copy-start
  163.7 0.7 collective-permute-start.1
  164.4 3.5 copy-start
  169.1 0.7 collective-permute-start.1
  169.8 3.5 copy-start
  174.5 0.7 collective-permute-start.1
  175.2 3.5 copy-start
  179.8 0.7 collective-permute-start.1
  180.5 3.5 copy-start
  185.2 0.7 collective-permute-start.1
  185.9 3.5 copy-start
  190.6 0.7 collective-permute-start.1
  191.3 3.5 copy-start
  196.0 0.7 collective-permute-start.1
  196.7 3.5 copy-start
  201.3 0.7 collective-permute-start.1
  206.7 0.7 collective-permute-start.1
  212.1 0.7 collective-permute-start.1
  212.8 3.5 copy-start
  217.4 0.7 collective-permute-start.1
  222.8 0.7 collective-permute-start.1
  228.2 300.8 %collective-permute-start.5 = (f32[2,4,8,1024]{3,2,1,0:T(8,128)S(1)}, f32[2,4,8,1024]{3,2,1,0:T(8,128)S(1)}, u32[]{:S(2)}, u32[]{:S(2)}) collective-permute-start(f32[2,4,8,1024]{3,2,1,0:T(8,128)S(1)} %get-tuple-element.378), channel_id=1, source_target_pairs={{0,8},{16,24},{32,40},{48,56},{64,72},{80,88},{96,104},{112,120},{... | collective-permute-start | bytes 786440 | tf_op jit(solution)/shard_map/ppermute | solution.py:91
  (20 other events, 66.5 us)
Sparse Core Ops, SparseCore 0:
  22.4 37.9 all-gather.1
